TPU v7x, 32 devices: a whole 2x2x4 slice. The times are simulated.
32 devices in a mesh: leaf: 4 (over y, x), src: 8 (over z, core).
Axes of the slice: x: 2, y: 2, z: 4, core: 2. Of those that a mesh axis runs over, the one named last changes fastest.
Arguments:
- src_cells: int32 [1024], P('src'), may hold values from 0 to 2047
- rec_cells: int32 [512], P('leaf'), may hold values from 0 to 511
- residual: float32 [1024, 512], P('src', 'leaf'), may hold values from -6 to 6
- pattern: int32 [12, 2], P('leaf'), may hold values 0 or 1
- leaf_lower: bfloat16 [2048, 512], P('leaf'), may hold values from -0.1875 to 0.1875
- leaf_upper: bfloat16 [2048, 512], P('leaf'), may hold values from -0.1875 to 0.1875
- leaf_inv: bfloat16 [16, 128, 128], P('leaf'), may hold values from -0.5 to 0.5
- anc_lower: bfloat16 [1024, 512], P('leaf'), may hold values from -0.125 to 0.125
- anc_upper: bfloat16 [2048, 256], P('leaf'), may hold values from -0.375 to 0.375
- sep_inv: bfloat16 [8, 128, 128], P('leaf'), may hold values from -0.5 to 0.5
- sep_lower: bfloat16 [8, 256, 128], P('leaf'), may hold values from -0.25 to 0.25
- sep_upper: bfloat16 [8, 128, 256], P('leaf'), may hold values from -0.375 to 0.375
Outputs:
- forward_field: float32 [1024, 2048], P('src', 'leaf')
- adjoint_field: float32 [1024, 2048], P('src', 'leaf')
- gradient: float32 [2048], P(('leaf', 'src'))
Inputs may be any that keep to these rules, and one draw needn't show every extreme that they name: src_cells holds 512 d + c for a source in interior cell c of subdomain d. rec_cells holds a receiver's cell within the subdomain of its block of 128 entries.
All inputs are finite; a program needn't handle non-finite values. No bound on the sum of `pattern` on one device may be relied on, other than what follows from the above.
Results may differ from a plain program's by a relative error of at most 0.0068.
Values may be sent and summed in bfloat16 or wider, within the bound.
No kernel may reach another device: no remote copies, remote signals or barrier semaphores. Data moves between devices by JAX's collectives and lax.ppermute only.
A program may use at most 64 MiB of HBM per device.

v0:
```python
import math
import jax
import jax.numpy as jnp
from jax import lax
from jax.sharding import PartitionSpec as P


def across(former, latter):
    return lax.dot_general(
        former, latter, (((1,), (1,)), ((), ())), preferred_element_type=jnp.float32
    )


def plain_dot(former, latter):
    return jnp.dot(former, latter, preferred_element_type=jnp.float32)


def as_half(values):
    return values.astype(jnp.bfloat16)


def lower_solve(right_side, lower, block_size, block_count):
    solved = []
    for index in range(block_count):
        segment = right_side[:, index * block_size : (index + 1) * block_size]
        if index:
            earlier = as_half(jnp.concatenate(solved, axis=1))
            segment = segment - across(
                earlier, lower[index * block_size : (index + 1) * block_size, : index * block_size]
            )
        solved.append(segment)
    return jnp.concatenate(solved, axis=1)


def upper_solve(right_side, upper, inverse, block_size, block_count):
    behind = []
    for index in reversed(range(block_count)):
        segment = right_side[:, index * block_size : (index + 1) * block_size]
        if behind:
            segment = segment - across(
                as_half(jnp.concatenate(behind, axis=1)),
                upper[index * block_size : (index + 1) * block_size, (index + 1) * block_size :],
            )
        behind.insert(0, across(as_half(segment), inverse[index]))
    return jnp.concatenate(behind, axis=1)


def upper_t_solve(right_side, upper, inverse, block_size, block_count):
    solved = []
    for index in range(block_count):
        segment = right_side[:, index * block_size : (index + 1) * block_size]
        if index:
            earlier = as_half(jnp.concatenate(solved, axis=1))
            segment = segment - plain_dot(
                earlier, upper[: index * block_size, index * block_size : (index + 1) * block_size]
            )
        solved.append(plain_dot(as_half(segment), inverse[index]))
    return jnp.concatenate(solved, axis=1)


def lower_t_solve(right_side, lower, block_size, block_count):
    behind = []
    for index in reversed(range(block_count)):
        segment = right_side[:, index * block_size : (index + 1) * block_size]
        if behind:
            segment = segment - plain_dot(
                as_half(jnp.concatenate(behind, axis=1)),
                lower[(index + 1) * block_size :, index * block_size : (index + 1) * block_size],
            )
        behind.insert(0, segment)
    return jnp.concatenate(behind, axis=1)


def climb(starts, handlers, levels, block_size, device):
    contributions = list(starts)
    results = [[] for member in starts]
    for height in range(1, levels + 1):
        lowest = (height - 1) * block_size
        piece = jnp.stack([summed[:, lowest : lowest + block_size] for summed in contributions])
        gathered = lax.all_gather(piece[None], "leaf", axis=0, tiled=True)
        first = device >> height << height
        total = jnp.sum(lax.dynamic_slice_in_dim(gathered, first, 1 << height, 0), axis=0)
        owner = device % (1 << height) == 0
        member = 0
        node_value, coupling = handlers[member](height, total[member])
        results[member].append(node_value)
        contributions[member] = contributions[member] + jnp.where(
            owner, coupling, jnp.zeros_like(coupling)
        )
    return results


def descend(node_values, handlers, levels, block_size, device, sources):
    known = [jnp.zeros((sources, levels * block_size), jnp.float32) for member in node_values]
    for height in range(levels, 0, -1):
        outgoing = jnp.stack([as_half(handlers[0](height, known[0], node_values[0][height - 1]))])
        gathered = lax.all_gather(outgoing[None], "leaf", axis=0, tiled=True)
        owner_index = device >> height << height
        piece = lax.dynamic_index_in_dim(gathered, owner_index, 0, keepdims=False).astype(
            jnp.float32
        )
        known = [lax.dynamic_update_slice_in_dim(known[0], piece[0], (height - 1) * block_size, 1)]
    return known


def shards(
    src_cells,
    rec_cells,
    residual,
    pattern,
    leaf_lower,
    leaf_upper,
    leaf_inv,
    anc_lower,
    anc_upper,
    sep_inv,
    sep_lower,
    sep_upper,
):
    levels = lax.axis_size("leaf").bit_length() - 1
    device = lax.axis_index("leaf")
    block_size = leaf_inv.shape[1]
    block_count = leaf_inv.shape[0]
    cell_count = leaf_lower.shape[1]
    source_count = src_cells.shape[0]
    factor = 1.0 / math.sqrt(source_count * lax.axis_size("src"))
    present = pattern.astype(jnp.float32)

    def level_mask(height):
        level_row = present[height] * (jnp.arange(1, levels + 1) > height).astype(jnp.float32)
        return jnp.repeat(level_row, block_size)

    columns = lax.broadcasted_iota(jnp.int32, (source_count, cell_count), 1)
    forcing = (src_cells[:, None] - device * cell_count == columns).astype(jnp.float32)
    receiver_hits = (
        rec_cells[:, None] == lax.broadcasted_iota(jnp.int32, (rec_cells.shape[0], cell_count), 1)
    ).astype(jnp.float32)
    adjoint_rhs = jnp.dot(residual, receiver_hits, precision=lax.Precision.HIGHEST)

    def forward_up(height, summed):
        node_value = -summed
        return (node_value, across(as_half(node_value), sep_lower[height - 1]) * level_mask(height))

    def adjoint_up(height, summed):
        node_value = plain_dot(as_half(-summed), sep_inv[height - 1])
        return (
            node_value,
            plain_dot(as_half(node_value), sep_upper[height - 1]) * level_mask(height),
        )

    def forward_down(height, above, node_value):
        right_side = node_value - across(as_half(above * level_mask(height)), sep_upper[height - 1])
        return across(as_half(right_side), sep_inv[height - 1])

    def adjoint_down(height, above, node_value):
        return node_value - plain_dot(as_half(above * level_mask(height)), sep_lower[height - 1])

    base_mask = level_mask(0)
    y_leaf = lower_solve(forcing, leaf_lower, block_size, block_count)
    forward_start = across(as_half(y_leaf), anc_lower) * base_mask
    z_leaf = upper_t_solve(adjoint_rhs, leaf_upper, leaf_inv, block_size, block_count)
    adjoint_start = plain_dot(as_half(z_leaf), anc_upper) * base_mask
    forward_values = climb([forward_start], [forward_up], levels, block_size, device)
    forward_above = descend(
        forward_values, [forward_down], levels, block_size, device, source_count
    )[0]
    adjoint_values = climb([adjoint_start], [adjoint_up], levels, block_size, device)
    adjoint_above = descend(
        adjoint_values, [adjoint_down], levels, block_size, device, source_count
    )[0]
    forward_remain = y_leaf - across(as_half(forward_above * base_mask), anc_upper)
    forward_field = upper_solve(forward_remain, leaf_upper, leaf_inv, block_size, block_count)
    adjoint_remain = z_leaf - plain_dot(as_half(adjoint_above * base_mask), anc_lower)
    adjoint_field = lower_t_solve(adjoint_remain, leaf_lower, block_size, block_count)
    partial_gradient = jnp.sum(forward_field * adjoint_field, axis=0)
    gradient = lax.psum_scatter(partial_gradient, "src", scatter_dimension=0, tiled=True) * factor
    return (forward_field, adjoint_field, gradient)


def solution(mesh):
    in_specs = (
        P("src"),
        P("leaf"),
        P("src", "leaf"),
        P("leaf", None),
        P("leaf", None),
        P("leaf", None),
        P("leaf", None, None),
        P("leaf", None),
        P("leaf", None),
        P("leaf", None, None),
        P("leaf", None, None),
        P("leaf", None, None),
    )
    out_specs = (P("src", "leaf"), P("src", "leaf"), P(("leaf", "src")))
    return jax.shard_map(shards, mesh=mesh, in_specs=in_specs, out_specs=out_specs, check_vma=False)
```

profile of v0, /device:TPU:0, one launch (start us, length us, event | category | flops | bytes accessed | tf_op | source)
XLA Modules:
  0.0 98.7 jit_solution(13294854775724279794)
XLA Ops:
  0.7 0.7 broadcast_subtract_fusion
  1.4 0.9 fusion.189
  2.4 0.1 fusion.190
  2.5 0.2 convolution_subtract_fusion.5
  2.7 0.7 copy-done.9
  3.4 0.2 slice_reduce_fusion
  3.7 0.2 convolution_multiply_fusion.1
  4.0 10.6 %all-gather = f32[512,128]{1,0:T(8,128)S(1)} all-gather(f32[128,128]{1,0:T(8,128)S(1)} %slice.198), channel_id=2, replica_groups=mesh['leaf'=4,'src'=8] {'leaf'}, dimensions={0}, use_global_device_ids=true | all-gather | bytes 327680 | tf_op jit(solution)/shard_map/all_gather | solution.py:80
  14.6 0.4 convolution_bitcast_fusion
  15.0 0.5 copy-done.3
  15.5 0.2 fusion.180
  15.7 0.3 fusion.181
  16.0 0.4 fusion.184
  16.4 0.4 fusion.13
  16.8 0.2 convolution_multiply_fusion
  17.0 9.0 %all-gather.4 = f32[512,128]{1,0:T(8,128)S(1)} all-gather(f32[128,128]{1,0:T(8,128)S(1)} %slice.210), channel_id=6, replica_groups=mesh['leaf'=4,'src'=8] {'leaf'}, dimensions={0}, use_global_device_ids=true | all-gather | bytes 327680 | tf_op jit(solution)/shard_map/all_gather | solution.py:80
  26.0 0.8 copy-done.4
  26.8 0.1 fusion.121
  27.0 0.1 fusion.91
  27.1 0.8 copy-done.1
  27.9 0.2 fusion.98
  28.2 8.1 %all-gather.1 = f32[512,128]{1,0:T(8,128)S(1)} all-gather(f32[128,128]{1,0:T(8,128)S(1)} %get-tuple-element.16), channel_id=3, replica_groups=mesh['leaf'=4,'src'=8] {'leaf'}, dimensions={0}, use_global_device_ids=true | all-gather | bytes 327680 | tf_op jit(solution)/shard_map/all_gather | solution.py:80
  36.4 0.3 convolution_convert_fusion.1
  36.6 8.7 %all-gather.2 = bf16[512,128]{1,0:T(8,128)(2,1)S(1)} all-gather(bf16[128,128]{1,0:T(8,128)(2,1)S(1)} %convolution_convert_fusion.1), channel_id=4, replica_groups=mesh['leaf'=4,'src'=8] {'leaf'}, dimensions={0}, use_global_device_ids=true | all-gather | bytes 163840 | tf_op jit(solution)/shard_map/all_gather | solution.py:97
  45.4 0.3 convolution_convert_fusion
  45.7 7.3 %all-gather.3 = bf16[512,128]{1,0:T(8,128)(2,1)S(1)} all-gather(bf16[128,128]{1,0:T(8,128)(2,1)S(1)} %convolution_convert_fusion), channel_id=5, replica_groups=mesh['leaf'=4,'src'=8] {'leaf'}, dimensions={0}, use_global_device_ids=true | all-gather | bytes 163840 | tf_op jit(solution)/shard_map/all_gather | solution.py:97
  53.0 0.2 convolution_subtract_fusion.1
  53.2 0.1 fusion.193
  53.3 0.3 fusion.194
  53.6 0.3 fusion.197
  53.9 0.3 fusion.10
  54.2 9.2 %all-gather.5 = f32[512,128]{1,0:T(8,128)S(1)} all-gather(f32[128,128]{1,0:T(8,128)S(1)} %get-tuple-element.15), channel_id=7, replica_groups=mesh['leaf'=4,'src'=8] {'leaf'}, dimensions={0}, use_global_device_ids=true | all-gather | bytes 327680 | tf_op jit(solution)/shard_map/all_gather | solution.py:80
  63.5 0.1 fusion.122
  63.6 0.2 fusion.5
  63.7 7.3 %all-gather.6 = bf16[512,128]{1,0:T(8,128)(2,1)S(1)} all-gather(bf16[128,128]{1,0:T(8,128)(2,1)S(1)} %fusion.5), channel_id=8, replica_groups=mesh['leaf'=4,'src'=8] {'leaf'}, dimensions={0}, use_global_device_ids=true | all-gather | bytes 163840 | tf_op jit(solution)/shard_map/all_gather | solution.py:97
  71.1 0.1 fusion.6
  71.2 8.6 %all-gather.7 = bf16[512,128]{1,0:T(8,128)(2,1)S(1)} all-gather(bf16[128,128]{1,0:T(8,128)(2,1)S(1)} %fusion.6), channel_id=9, replica_groups=mesh['leaf'=4,'src'=8] {'leaf'}, dimensions={0}, use_global_device_ids=true | all-gather | bytes 163840 | tf_op jit(solution)/shard_map/all_gather | solution.py:97
  79.9 0.3 convolution_subtract_fusion
  80.1 0.2 fusion.191
  80.4 0.2 fusion.192
  80.6 0.2 convolution_subtract_fusion.8
  80.8 0.1 multiply_reduce_fusion
  81.0 0.8 copy.21
  81.8 0.8 copy.22
  82.7 13.6 %all-reduce.2 = f32[512]{0:T(512)S(1)} all-reduce(f32[512]{0:T(512)S(1)} %get-tuple-element.12), channel_id=10, replica_groups=mesh['leaf'=4,'src'=8] {'src'}, use_global_device_ids=true, to_apply=%region_5.6.clone | all-reduce | flops 512 | bytes 4096
  96.3 0.7 copy-done.11
  96.9 0.6 dynamic-slice
  98.1 0.6 dynamic-slice_multiply_fusion
  (42 shorter events, 0.5 us)
Async XLA Ops:
  0.6 16.1 %copy-start = (bf16[512,256]{1,0:T(8,128)(2,1)S(1)}, bf16[512,256]{1,0:T(8,128)(2,1)}, u32[]{:S(2)}) copy-start(bf16[512,256]{1,0:T(8,128)(2,1)} %param.20) | copy-start | bytes 786436
  0.6 1.7 %copy-start.7 = (bf16[512,512]{1,0:T(8,128)(2,1)S(1)}, bf16[512,512]{1,0:T(8,128)(2,1)}, u32[]{:S(2)}) copy-start(bf16[512,512]{1,0:T(8,128)(2,1)} %param.16) | copy-start | bytes 1572868
  2.5 1.2 %copy-start.5 = (bf16[256,512]{1,0:T(8,128)(2,1)S(1)}, bf16[256,512]{1,0:T(8,128)(2,1)}, u32[]{:S(2)}) copy-start(bf16[256,512]{1,0:T(8,128)(2,1)} %param.19) | copy-start | bytes 786436
  2.7 0.7 copy-start.9
  3.7 10.9 %copy-start.8 = (f32[128,128]{1,0:T(8,128)S(1)}, f32[128,128]{1,0:T(8,128)}, u32[]{:S(2)}) copy-start(f32[128,128]{1,0:T(8,128)} %param.14) | copy-start | bytes 196612
  3.7 10.9 %copy-start.10 = (s32[128]{0:T(128)S(1)}, s32[128]{0:T(128)}, u32[]{:S(2)}) copy-start(s32[128]{0:T(128)} %param.13) | copy-start | bytes 1540
  3.9 11.7 %copy-start.6 = (bf16[512,512]{1,0:T(8,128)(2,1)S(1)}, bf16[512,512]{1,0:T(8,128)(2,1)}, u32[]{:S(2)}) copy-start(bf16[512,512]{1,0:T(8,128)(2,1)} %param.17) | copy-start | bytes 1572868
  14.6 0.9 copy-start.3
  26.0 0.8 copy-start.4
  26.0 0.9 copy-start.2
  27.0 0.9 copy-start.1
  96.2 0.7 copy-start.11
where the time goes:
time: 99.2 us; the launch traced here: 98.7 us
  blocking collectives  82.3 us (83%)
  matrix products  6.91 us (7%)
  local copies, waits for them, and re-layouts  6.16 us (6%)
  between operations  1.7 us (2%)
  other arithmetic  1.61 us (2%)
    all_gather x4, blocking collectives, climb(): gathered = lax.all_gather(piece[None], 'leaf', axis=0, tiled=True)  36.8 us
    all_gather x4, blocking collectives, descend(): gathered = lax.all_gather(outgoing[None], 'leaf', axis=0, tiled=True)  31.9 us
    unnamed x1, blocking collectives  13.6 us
    unnamed x27, local copies, waits for them, and re-layouts  5.69 us
    dot_general x12, matrix products, across(): lax.dot_general(former, latter, (((1,), (1,)), ((), ())), preferred_eleme...  3.42 us
    dot_general x14, matrix products, plain_dot(): return jnp.dot(former, latter, preferred_element_type=jnp.float32)  3.11 us

commit v1 on v0

--- a/solution.py
+++ b/solution.py
@@ -77,7 +77,30 @@
     for height in range(1, levels + 1):
         lowest = (height - 1) * block_size
         piece = jnp.stack([summed[:, lowest : lowest + block_size] for summed in contributions])
-        gathered = lax.all_gather(piece[None], "leaf", axis=0, tiled=True)
+        devices, mine, extent = (
+            lax.axis_size("leaf"),
+            lax.axis_index("leaf"),
+            piece[None].shape[0],
+        )
+        upward = [(i, (i + 1) % devices) for i in range(devices)]
+        behind_2 = [(i, (i - 1) % devices) for i in range(devices)]
+        gathered = jnp.zeros(
+            (*piece[None].shape[:0], devices * extent, *piece[None].shape[0 + 1 :]),
+            piece[None].dtype,
+        )
+        gathered = lax.dynamic_update_slice_in_dim(gathered, piece[None], mine * extent, axis=0)
+        from_left = from_right = piece[None]
+        halfway = devices // 2
+        for step in range(1, halfway + 1):
+            from_left = lax.ppermute(from_left, "leaf", upward)
+            gathered = lax.dynamic_update_slice_in_dim(
+                gathered, from_left, (mine - step) % devices * extent, axis=0
+            )
+            if step < devices - halfway:
+                from_right = lax.ppermute(from_right, "leaf", behind_2)
+                gathered = lax.dynamic_update_slice_in_dim(
+                    gathered, from_right, (mine + step) % devices * extent, axis=0
+                )
         first = device >> height << height
         total = jnp.sum(lax.dynamic_slice_in_dim(gathered, first, 1 << height, 0), axis=0)
         owner = device % (1 << height) == 0

time: 99.2 us -> 89.4 us (0.901)
  blocking collectives: 82.3 us -> 45.7 us
  starting transfers between devices: 0 us -> 17.8 us
  waiting for transfers between devices: 0 us -> 7.1 us
  local copies, waits for them, and re-layouts: 6.16 us -> 7.94 us
    all_gather x4 -> x0, blocking collectives: 36.8 us -> none  [climb(): gathered = lax.all_gather(piece[None], 'leaf', axis=0, tiled=True)]
    ppermute x0 -> x12, starting transfers between devices: none -> 17.8 us  [the longest x8 9.63 us: climb(): from_left = lax.ppermute(from_left, 'leaf', upward)]
    ppermute x0 -> x12, waiting for transfers between devices: none -> 7.1 us  [the longest x8 6.5 us: climb(): from_left = lax.ppermute(from_left, 'leaf', upward)]
    unnamed x27 -> x25, local copies, waits for them, and re-layouts: 5.69 us -> 6.41 us
  transfers between devices with their start and end apart: 0 -> 12, of which waited for: 0 -> 5; matrix products, arithmetic and copies ran while one was open for 0% -> 6% of each run, Pallas kernels for 0% -> 0%
where the time goes in v1:
time: 89.4 us; the launch traced here: 89 us
  blocking collectives  45.7 us (51%)
  starting transfers between devices  17.8 us (20%)
  local copies, waits for them, and re-layouts  7.94 us (9%)
  waiting for transfers between devices  7.1 us (8%)
  matrix products  6.92 us (8%)
  between operations  1.87 us (2%)
  other arithmetic  1.65 us (2%)
    all_gather x4, blocking collectives, descend(): gathered = lax.all_gather(outgoing[None], 'leaf', axis=0, tiled=True)  32.1 us
    unnamed x1, blocking collectives  13.6 us
    ppermute x8, starting transfers between devices, climb(): from_left = lax.ppermute(from_left, 'leaf', upward)  9.63 us
    ppermute x4, starting transfers between devices, climb(): from_right = lax.ppermute(from_right, 'leaf', behind_2)  8.18 us
    ppermute x8, waiting for transfers between devices, climb(): from_left = lax.ppermute(from_left, 'leaf', upward)  6.5 us
    unnamed x25, local copies, waits for them, and re-layouts  6.41 us
    dot_general x12, matrix products, across(): lax.dot_general(former, latter, (((1,), (1,)), ((), ())), preferred_eleme...  3.43 us
    dot_general x14, matrix products, plain_dot(): return jnp.dot(former, latter, preferred_element_type=jnp.float32)  3.12 us
  transfers between devices with their start and end apart: 12, of which 5 were waited for; matrix products, arithmetic and copies ran while one was open for 6% of the time, Pallas kernels for 0%

profile of v1, /device:TPU:0, one launch (start us, length us, event | category | flops | bytes accessed | tf_op | source)
XLA Modules:
  0.0 89.0 jit_solution(12822596794534241850)
XLA Ops:
  0.7 0.7 broadcast_subtract_fusion
  1.5 0.9 %fusion.196 = (bf16[128,128]{0,1:T(8,128)(2,1)S(1)}, f32[128,128]{0,1:T(8,128)S(1)}) fusion(bf16[512,512]{1,0:T(8,128)(2,1)} %param.16, f32[128,512]{0,1:T(8,128)S(1)} %fusion.15), kind=kOutput, calls=%fused_computation.229 | convolution fusion | flops 4227072 | bytes 229376 | tf_op jit(solution)/shard_map/dot_general | solution.py:9
  2.7 0.5 copy-done.9
  3.5 0.2 convolution_multiply_fusion.1
  3.8 3.0 %collective-permute-start = (f32[1,1,128,128]{3,2,1,0:T(8,128)S(1)}, f32[1,1,128,128]{3,2,1,0:T(8,128)S(1)}, u32[]{:S(2)}, u32[]{:S(2)}) collective-permute-start(f32[1,1,128,128]{3,2,1,0:T(8,128)S(1)} %slice_bitcast_fusion.1), channel_id=1, source_target_pairs={{0,8},{8,16},{16,24},{24,0},{1,9},{9,17},{17,25},{25,1},{2,10},{10... | collective-permute-start | bytes 196616 | tf_op jit(solution)/shard_map/ppermute | solution.py:95
  6.8 1.0 %collective-permute-start.1 = (f32[1,1,128,128]{3,2,1,0:T(8,128)S(1)}, f32[1,1,128,128]{3,2,1,0:T(8,128)S(1)}, u32[]{:S(2)}, u32[]{:S(2)}) collective-permute-start(f32[1,1,128,128]{3,2,1,0:T(8,128)S(1)} %slice_bitcast_fusion.1), channel_id=1, source_target_pairs={{0,24},{8,0},{16,8},{24,16},{1,25},{9,1},{17,9},{25,17},{2,26},{10... | collective-permute-start | bytes 196616 | tf_op jit(solution)/shard_map/ppermute | solution.py:100
  7.8 0.4 convolution_bitcast_fusion
  8.4 0.3 fusion.186
  8.8 0.4 fusion.189
  9.2 0.4 fusion.12
  9.5 0.6 copy-done.1
  10.1 0.2 convolution_multiply_fusion
  10.4 1.1 %collective-permute-start.6 = (f32[1,1,128,128]{3,2,1,0:T(8,128)S(1)}, f32[1,1,128,128]{3,2,1,0:T(8,128)}, u32[]{:S(2)}, u32[]{:S(2)}) collective-permute-start(f32[1,1,128,128]{3,2,1,0:T(8,128)S(1)} %slice_bitcast_fusion), channel_id=1, source_target_pairs={{0,8},{8,16},{16,24},{24,0},{1,9},{9,17},{17,25},{25,1},{2,10},{10... | collective-permute-start | bytes 196616 | tf_op jit(solution)/shard_map/ppermute | solution.py:95
  11.4 1.9 %collective-permute-start.7 = (f32[1,1,128,128]{3,2,1,0:T(8,128)S(1)}, f32[1,1,128,128]{3,2,1,0:T(8,128)S(1)}, u32[]{:S(2)}, u32[]{:S(2)}) collective-permute-start(f32[1,1,128,128]{3,2,1,0:T(8,128)S(1)} %slice_bitcast_fusion), channel_id=1, source_target_pairs={{0,24},{8,0},{16,8},{24,16},{1,25},{9,1},{17,9},{25,17},{2,26},{10... | collective-permute-start | bytes 196616 | tf_op jit(solution)/shard_map/ppermute | solution.py:100
  13.5 0.8 copy-done.2
  14.6 1.2 %dynamic-slice = u32[1]{0:T(128)} dynamic-slice(u32[32]{0:T(128)} %constant.97, u32[]{:T(128)S(6)} %add.108), dynamic_slice_sizes={1} | dynamic-slice | bytes 12
  16.5 0.5 collective-permute-start.2
  17.0 2.9 %collective-permute-start.8 = (f32[1,1,128,128]{3,2,1,0:T(8,128)}, f32[1,1,128,128]{3,2,1,0:T(8,128)S(1)}, u32[]{:S(2)}, u32[]{:S(2)}) collective-permute-start(f32[1,1,128,128]{3,2,1,0:T(8,128)} %collective-permute-done.6), channel_id=1, source_target_pairs={{0,8},{8,16},{16,24},{24,0},{1,9},{9,17},{17,25},{25,1},{2,10},{10... | collective-permute-start | bytes 196616 | tf_op jit(solution)/shard_map/ppermute | solution.py:95
  19.9 0.9 constant_dynamic-update-slice_fusion.6
  20.9 0.8 collective-permute-done.2
  22.1 2.8 %collective-permute-start.4 = (f32[1,1,128,128]{3,2,1,0:T(8,128)S(1)}, f32[1,1,128,128]{3,2,1,0:T(8,128)S(1)}, u32[]{:S(2)}, u32[]{:S(2)}) collective-permute-start(f32[1,1,128,128]{3,2,1,0:T(8,128)S(1)} %get-tuple-element.15), channel_id=1, source_target_pairs={{0,24},{8,0},{16,8},{24,16},{1,25},{9,1},{17,9},{25,17},{2,26},{10... | collective-permute-start | bytes 196616 | tf_op jit(solution)/shard_map/ppermute | solution.py:100
  25.0 0.8 copy-done.5
  25.9 0.8 copy-done.3
  26.9 0.5 collective-permute-start.9
  27.4 2.4 %collective-permute-start.10 = (f32[1,1,128,128]{3,2,1,0:T(8,128)S(1)}, f32[1,1,128,128]{3,2,1,0:T(8,128)S(1)}, u32[]{:S(2)}, u32[]{:S(2)}) collective-permute-start(f32[1,1,128,128]{3,2,1,0:T(8,128)S(1)} %get-tuple-element.13), channel_id=1, source_target_pairs={{0,24},{8,0},{16,8},{24,16},{1,25},{9,1},{17,9},{25,17},{2,26},{10... | collective-permute-start | bytes 196616 | tf_op jit(solution)/shard_map/ppermute | solution.py:100
  29.9 0.5 collective-permute-start.5
  30.4 2.0 %collective-permute-done.9 = f32[1,1,128,128]{3,2,1,0:T(8,128)S(1)} collective-permute-done((f32[1,1,128,128]{3,2,1,0:T(8,128)S(1)}, f32[1,1,128,128]{3,2,1,0:T(8,128)S(1)}, u32[]{:S(2)}, u32[]{:S(2)}) %collective-permute-start.9) | collective-permute-done | bytes 65568 | tf_op jit(solution)/shard_map/ppermute | solution.py:95
  32.4 0.9 %collective-permute-start.11 = (f32[1,1,128,128]{3,2,1,0:T(8,128)S(1)}, f32[1,1,128,128]{3,2,1,0:T(8,128)S(1)}, u32[]{:S(2)}, u32[]{:S(2)}) collective-permute-start(f32[1,1,128,128]{3,2,1,0:T(8,128)S(1)} %collective-permute-done.9), channel_id=1, source_target_pairs={{0,8},{8,16},{16,24},{24,0},{1,9},{9,17},{17,25},{25,1},{2,10},{10... | collective-permute-start | bytes 196616 | tf_op jit(solution)/shard_map/ppermute | solution.py:95
  33.4 0.6 collective-permute-done.10
  34.0 1.0 %collective-permute-done.5 = f32[1,1,128,128]{3,2,1,0:T(8,128)S(1)} collective-permute-done((f32[1,1,128,128]{3,2,1,0:T(8,128)S(1)}, f32[1,1,128,128]{3,2,1,0:T(8,128)S(1)}, u32[]{:S(2)}, u32[]{:S(2)}) %collective-permute-start.5) | collective-permute-done | bytes 65568 | tf_op jit(solution)/shard_map/ppermute | solution.py:95
  35.0 2.6 %collective-permute-done.11 = f32[1,1,128,128]{3,2,1,0:T(8,128)S(1)} collective-permute-done((f32[1,1,128,128]{3,2,1,0:T(8,128)S(1)}, f32[1,1,128,128]{3,2,1,0:T(8,128)S(1)}, u32[]{:S(2)}, u32[]{:S(2)}) %collective-permute-start.11) | collective-permute-done | bytes 65568 | tf_op jit(solution)/shard_map/ppermute | solution.py:95
  37.8 8.9 %all-gather.2 = bf16[512,128]{1,0:T(8,128)(2,1)S(1)} all-gather(bf16[128,128]{1,0:T(8,128)(2,1)S(1)} %fusion.4), channel_id=4, replica_groups=mesh['leaf'=4,'src'=8] {'leaf'}, dimensions={0}, use_global_device_ids=true | all-gather | bytes 163840 | tf_op jit(solution)/shard_map/all_gather | solution.py:120
  46.8 7.3 %all-gather.3 = bf16[512,128]{1,0:T(8,128)(2,1)S(1)} all-gather(bf16[128,128]{1,0:T(8,128)(2,1)S(1)} %fusion.5), channel_id=5, replica_groups=mesh['leaf'=4,'src'=8] {'leaf'}, dimensions={0}, use_global_device_ids=true | all-gather | bytes 163840 | tf_op jit(solution)/shard_map/all_gather | solution.py:120
  54.1 0.3 convolution_subtract_fusion
  54.7 0.3 convolution_convert_fusion.1
  55.0 8.7 %all-gather = bf16[512,128]{1,0:T(8,128)(2,1)S(1)} all-gather(bf16[128,128]{1,0:T(8,128)(2,1)S(1)} %convolution_convert_fusion.1), channel_id=2, replica_groups=mesh['leaf'=4,'src'=8] {'leaf'}, dimensions={0}, use_global_device_ids=true | all-gather | bytes 163840 | tf_op jit(solution)/shard_map/all_gather | solution.py:120
  63.7 0.3 convolution_convert_fusion
  64.0 7.3 %all-gather.1 = bf16[512,128]{1,0:T(8,128)(2,1)S(1)} all-gather(bf16[128,128]{1,0:T(8,128)(2,1)S(1)} %convolution_convert_fusion), channel_id=3, replica_groups=mesh['leaf'=4,'src'=8] {'leaf'}, dimensions={0}, use_global_device_ids=true | all-gather | bytes 163840 | tf_op jit(solution)/shard_map/all_gather | solution.py:120
  71.2 0.2 convolution_subtract_fusion.1
  71.6 0.3 fusion.199
  71.9 0.3 fusion.202
  72.2 0.3 fusion.9
  72.5 0.2 fusion.195
  72.7 0.2 convolution_subtract_fusion.8
  73.1 0.8 copy.21
  74.0 0.8 copy.22
  74.8 13.6 %all-reduce.2 = f32[512]{0:T(512)S(1)} all-reduce(f32[512]{0:T(512)S(1)} %get-tuple-element.16), channel_id=6, replica_groups=mesh['leaf'=4,'src'=8] {'src'}, use_global_device_ids=true, to_apply=%region_5.6.clone | all-reduce | flops 512 | bytes 4096
  88.4 0.6 dynamic-slice_multiply_fusion
  (79 shorter events, 3.0 us)
Async XLA Ops:
  0.6 2.9 %copy-start = (bf16[256,512]{1,0:T(8,128)(2,1)S(1)}, bf16[256,512]{1,0:T(8,128)(2,1)}, u32[]{:S(2)}) copy-start(bf16[256,512]{1,0:T(8,128)(2,1)} %param.19) | copy-start | bytes 786436
  0.6 1.7 %copy-start.7 = (bf16[512,512]{1,0:T(8,128)(2,1)S(1)}, bf16[512,512]{1,0:T(8,128)(2,1)}, u32[]{:S(2)}) copy-start(bf16[512,512]{1,0:T(8,128)(2,1)} %param.16) | copy-start | bytes 1572868
  2.5 0.7 copy-start.9
  3.5 4.9 %copy-start.6 = (bf16[512,512]{1,0:T(8,128)(2,1)S(1)}, bf16[512,512]{1,0:T(8,128)(2,1)}, u32[]{:S(2)}) copy-start(bf16[512,512]{1,0:T(8,128)(2,1)} %param.17) | copy-start | bytes 1572868
  3.7 4.1 %copy-start.8 = (f32[128,128]{1,0:T(8,128)S(1)}, f32[128,128]{1,0:T(8,128)}, u32[]{:S(2)}) copy-start(f32[128,128]{1,0:T(8,128)} %param.14) | copy-start | bytes 196612
  3.8 4.1 %copy-start.10 = (s32[128]{0:T(128)S(1)}, s32[128]{0:T(128)}, u32[]{:S(2)}) copy-start(s32[128]{0:T(128)} %param.13) | copy-start | bytes 1540
  3.8 4.4 %copy-start.4 = (bf16[4,128,128]{2,1,0:T(8,128)(2,1)S(1)}, bf16[4,128,128]{2,1,0:T(8,128)(2,1)}, u32[]{:S(2)}) copy-start(bf16[4,128,128]{2,1,0:T(8,128)(2,1)} %param.18) | copy-start | bytes 393220
  3.8 12.7 %collective-permute-start = (f32[1,1,128,128]{3,2,1,0:T(8,128)S(1)}, f32[1,1,128,128]{3,2,1,0:T(8,128)S(1)}, u32[]{:S(2)}, u32[]{:S(2)}) collective-permute-start(f32[1,1,128,128]{3,2,1,0:T(8,128)S(1)} %slice_bitcast_fusion.1), channel_id=1, source_target_pairs={{0,8},{8,16},{16,24},{24,0},{1,9},{9,17},{17,25},{25,1},{2,10},{10... | collective-permute-start | bytes 196616 | tf_op jit(solution)/shard_map/ppermute | solution.py:95
  6.8 14.0 %collective-permute-start.1 = (f32[1,1,128,128]{3,2,1,0:T(8,128)S(1)}, f32[1,1,128,128]{3,2,1,0:T(8,128)S(1)}, u32[]{:S(2)}, u32[]{:S(2)}) collective-permute-start(f32[1,1,128,128]{3,2,1,0:T(8,128)S(1)} %slice_bitcast_fusion.1), channel_id=1, source_target_pairs={{0,24},{8,0},{16,8},{24,16},{1,25},{9,1},{17,9},{25,17},{2,26},{10... | collective-permute-start | bytes 196616 | tf_op jit(solution)/shard_map/ppermute | solution.py:100
  9.2 1.0 %copy-start.1 = (bf16[512,256]{1,0:T(8,128)(2,1)S(1)}, bf16[512,256]{1,0:T(8,128)(2,1)}, u32[]{:S(2)}) copy-start(bf16[512,256]{1,0:T(8,128)(2,1)} %param.20) | copy-start | bytes 786436
  10.4 6.7 %collective-permute-start.6 = (f32[1,1,128,128]{3,2,1,0:T(8,128)S(1)}, f32[1,1,128,128]{3,2,1,0:T(8,128)}, u32[]{:S(2)}, u32[]{:S(2)}) collective-permute-start(f32[1,1,128,128]{3,2,1,0:T(8,128)S(1)} %slice_bitcast_fusion), channel_id=1, source_target_pairs={{0,8},{8,16},{16,24},{24,0},{1,9},{9,17},{17,25},{25,1},{2,10},{10... | collective-permute-start | bytes 196616 | tf_op jit(solution)/shard_map/ppermute | solution.py:95
  11.4 9.4 %collective-permute-start.7 = (f32[1,1,128,128]{3,2,1,0:T(8,128)S(1)}, f32[1,1,128,128]{3,2,1,0:T(8,128)S(1)}, u32[]{:S(2)}, u32[]{:S(2)}) collective-permute-start(f32[1,1,128,128]{3,2,1,0:T(8,128)S(1)} %slice_bitcast_fusion), channel_id=1, source_target_pairs={{0,24},{8,0},{16,8},{24,16},{1,25},{9,1},{17,9},{25,17},{2,26},{10... | collective-permute-start | bytes 196616 | tf_op jit(solution)/shard_map/ppermute | solution.py:100
  13.4 0.9 %copy-start.2 = (bf16[2,256,128]{2,1,0:T(8,128)(2,1)S(1)}, bf16[2,256,128]{2,1,0:T(8,128)(2,1)}, u32[]{:S(2)}) copy-start(bf16[2,256,128]{2,1,0:T(8,128)(2,1)} %param.22) | copy-start | bytes 393220
  16.5 5.2 %collective-permute-start.2 = (f32[1,1,128,128]{3,2,1,0:T(8,128)S(1)}, f32[1,1,128,128]{3,2,1,0:T(8,128)S(1)}, u32[]{:S(2)}, u32[]{:S(2)}) collective-permute-start(f32[1,1,128,128]{3,2,1,0:T(8,128)S(1)} %collective-permute-done), channel_id=1, source_target_pairs={{0,8},{8,16},{16,24},{24,0},{1,9},{9,17},{17,25},{25,1},{2,10},{10... | collective-permute-start | bytes 196616 | tf_op jit(solution)/shard_map/ppermute | solution.py:95
  17.0 7.9 %collective-permute-start.8 = (f32[1,1,128,128]{3,2,1,0:T(8,128)}, f32[1,1,128,128]{3,2,1,0:T(8,128)S(1)}, u32[]{:S(2)}, u32[]{:S(2)}) collective-permute-start(f32[1,1,128,128]{3,2,1,0:T(8,128)} %collective-permute-done.6), channel_id=1, source_target_pairs={{0,8},{8,16},{16,24},{24,0},{1,9},{9,17},{17,25},{25,1},{2,10},{10... | collective-permute-start | bytes 196616 | tf_op jit(solution)/shard_map/ppermute | solution.py:95
  22.0 7.9 %collective-permute-start.3 = (f32[1,1,128,128]{3,2,1,0:T(8,128)S(1)}, f32[1,1,128,128]{3,2,1,0:T(8,128)S(1)}, u32[]{:S(2)}, u32[]{:S(2)}) collective-permute-start(f32[1,1,128,128]{3,2,1,0:T(8,128)S(1)} %get-tuple-element.15), channel_id=1, source_target_pairs={{0,8},{8,16},{16,24},{24,0},{1,9},{9,17},{17,25},{25,1},{2,10},{10... | collective-permute-start | bytes 196616 | tf_op jit(solution)/shard_map/ppermute | solution.py:95
  22.1 11.2 %collective-permute-start.4 = (f32[1,1,128,128]{3,2,1,0:T(8,128)S(1)}, f32[1,1,128,128]{3,2,1,0:T(8,128)S(1)}, u32[]{:S(2)}, u32[]{:S(2)}) collective-permute-start(f32[1,1,128,128]{3,2,1,0:T(8,128)S(1)} %get-tuple-element.15), channel_id=1, source_target_pairs={{0,24},{8,0},{16,8},{24,16},{1,25},{9,1},{17,9},{25,17},{2,26},{10... | collective-permute-start | bytes 196616 | tf_op jit(solution)/shard_map/ppermute | solution.py:100
  24.9 0.8 copy-start.5
  25.8 0.9 %copy-start.3 = (bf16[2,128,256]{2,1,0:T(8,128)(2,1)S(1)}, bf16[2,128,256]{2,1,0:T(8,128)(2,1)}, u32[]{:S(2)}) copy-start(bf16[2,128,256]{2,1,0:T(8,128)(2,1)} %param.23) | copy-start | bytes 393220
  26.9 5.5 %collective-permute-start.9 = (f32[1,1,128,128]{3,2,1,0:T(8,128)S(1)}, f32[1,1,128,128]{3,2,1,0:T(8,128)S(1)}, u32[]{:S(2)}, u32[]{:S(2)}) collective-permute-start(f32[1,1,128,128]{3,2,1,0:T(8,128)S(1)} %get-tuple-element.13), channel_id=1, source_target_pairs={{0,8},{8,16},{16,24},{24,0},{1,9},{9,17},{17,25},{25,1},{2,10},{10... | collective-permute-start | bytes 196616 | tf_op jit(solution)/shard_map/ppermute | solution.py:95
  27.4 6.6 %collective-permute-start.10 = (f32[1,1,128,128]{3,2,1,0:T(8,128)S(1)}, f32[1,1,128,128]{3,2,1,0:T(8,128)S(1)}, u32[]{:S(2)}, u32[]{:S(2)}) collective-permute-start(f32[1,1,128,128]{3,2,1,0:T(8,128)S(1)} %get-tuple-element.13), channel_id=1, source_target_pairs={{0,24},{8,0},{16,8},{24,16},{1,25},{9,1},{17,9},{25,17},{2,26},{10... | collective-permute-start | bytes 196616 | tf_op jit(solution)/shard_map/ppermute | solution.py:100
  29.9 5.2 %collective-permute-start.5 = (f32[1,1,128,128]{3,2,1,0:T(8,128)S(1)}, f32[1,1,128,128]{3,2,1,0:T(8,128)S(1)}, u32[]{:S(2)}, u32[]{:S(2)}) collective-permute-start(f32[1,1,128,128]{3,2,1,0:T(8,128)S(1)} %collective-permute-done.3), channel_id=1, source_target_pairs={{0,8},{8,16},{16,24},{24,0},{1,9},{9,17},{17,25},{25,1},{2,10},{10... | collective-permute-start | bytes 196616 | tf_op jit(solution)/shard_map/ppermute | solution.py:95
  32.4 5.2 %collective-permute-start.11 = (f32[1,1,128,128]{3,2,1,0:T(8,128)S(1)}, f32[1,1,128,128]{3,2,1,0:T(8,128)S(1)}, u32[]{:S(2)}, u32[]{:S(2)}) collective-permute-start(f32[1,1,128,128]{3,2,1,0:T(8,128)S(1)} %collective-permute-done.9), channel_id=1, source_target_pairs={{0,8},{8,16},{16,24},{24,0},{1,9},{9,17},{17,25},{25,1},{2,10},{10... | collective-permute-start | bytes 196616 | tf_op jit(solution)/shard_map/ppermute | solution.py:95
